TPU v7x, 256 devices: a whole 4x4x8 slice. The times are simulated.
256 devices in a mesh: dp: 2 (over core), ctx: 8 (over y, z_lo), feat: 16 (over x, z_hi).
Axes of the slice: x: 4, y: 4, z: 8 (z_hi: 4, z_lo: 2; z = z_hi * 2 + z_lo), core: 2. Of those that a mesh axis runs over, the one named last changes fastest.
Arguments:
- out_grads: bfloat16 [2048, 28672], P(('dp', 'ctx'), 'feat'), may hold values from -6 to 6
- acts: bfloat16 [2048, 8192], P(('dp', 'ctx'), 'feat'), may hold values from -6 to 6
- domain_ids: int32 [2048], P(('dp', 'ctx')), may hold values from 0 to 7
- domain_weights: int32 [8], replicated, may hold values from 1 to 4
Outputs:
- grad_factor: bfloat16 [28672, 28672], P(('dp', 'ctx'), 'feat')
- act_factor: bfloat16 [8192, 8192], P(('dp', 'ctx'), 'feat')
All inputs are finite; a program needn't handle non-finite values.
Results may differ from a plain program's by a relative error of at most 0.003.
Values may be sent and summed in bfloat16 or wider, within the bound.
No kernel may reach another device: no remote copies, remote signals or barrier semaphores. Data moves between devices by JAX's collectives and lax.ppermute only.
A program may use at most 128 MiB of HBM per device.

v0:
```python
import jax
import jax.numpy as jnp
from jax import lax
from jax.sharding import PartitionSpec as P


def from_root(block, axis, owner):
    block = jnp.where(lax.axis_index(axis) == owner, block, jnp.zeros_like(block))
    return lax.psum(block, axis)


def weigh_rows(tok_ids, rows, domain_weights):
    labels = jnp.arange(domain_weights.shape[0], dtype=jnp.int32)
    match = tok_ids[:, None] == labels[None, :]
    tok_weight = jnp.sum(jnp.where(match, domain_weights[None, :], 0), axis=1).astype(jnp.float32)
    return (tok_weight[:, None] * rows.astype(jnp.float32)).astype(jnp.bfloat16)


def contract_tokens(left, right):
    return lax.dot_general(
        left, right, (((0,), (0,)), ((), ())), preferred_element_type=jnp.float32
    )


def local(out_grads, acts, domain_ids, domain_weights):
    group_size = lax.axis_size(("dp", "ctx"))
    inv_count = 1.0 / (out_grads.shape[0] * group_size)
    all_grads, all_acts, all_ids = (
        lax.all_gather(out_grads, ("dp", "ctx"), axis=0, tiled=True),
        lax.all_gather(acts, ("dp", "ctx"), axis=0, tiled=True),
        lax.all_gather(domain_ids, ("dp", "ctx"), axis=0, tiled=True),
    )
    tile_ratio = lax.axis_size("feat") // group_size
    first_root = lax.axis_index(("dp", "ctx")) * tile_ratio
    copy_grads = from_root(all_grads, "feat", first_root + 0)
    copy_acts = from_root(all_acts, "feat", first_root + 0)
    grad_sum = contract_tokens(copy_grads, weigh_rows(all_ids, all_grads, domain_weights))
    act_sum = contract_tokens(copy_acts, weigh_rows(all_ids, all_acts, domain_weights))
    grad_factor = (grad_sum * inv_count).astype(jnp.bfloat16)
    act_factor = (act_sum * inv_count).astype(jnp.bfloat16)
    return (grad_factor, act_factor)


def solution(mesh):
    in_specs = (P(("dp", "ctx"), "feat"), P(("dp", "ctx"), "feat"), P(("dp", "ctx")), P())
    out_specs = (P(("dp", "ctx"), "feat"), P(("dp", "ctx"), "feat"))
    return jax.shard_map(local, mesh=mesh, in_specs=in_specs, out_specs=out_specs, check_vma=False)
```

profile of v0, /device:TPU:41, one launch (start us, length us, event | category | flops | bytes accessed | tf_op | source)
XLA Modules:
  0.0 559.2 jit_solution(695061584460823528)
XLA Ops:
  7.2 0.0 all-gather.6.cloned.1.call-start
  7.2 0.7 all-gather.6.cloned.1.call-update
  7.9 0.0 all-gather.4.cloned.1.call-start
  7.9 0.7 all-gather.4.cloned.1.call-update
  8.6 0.0 all-reduce.3.cloned.1.call-start
  8.7 39.6 %all-gather.6.cloned.1.call-done = bf16[2048,512]{1,0:T(8,128)(2,1)} async-done(((bf16[128,512]{1,0:T(8,128)(2,1)}), bf16[2048,512]{1,0:T(8,128)(2,1)}) %all-gather.6.cloned.1.call-update) | async-done | bytes 2097168 | tf_op jit(solution)/shard_map/all_gather | solution.py:30
  48.3 1.5 broadcast_select_fusion.1
  49.8 51.1 %all-gather.4.cloned.1.call-done = bf16[2048,1792]{1,0:T(8,128)(2,1)} async-done(((bf16[128,1792]{1,0:T(8,128)(2,1)}), bf16[2048,1792]{1,0:T(8,128)(2,1)}) %all-gather.4.cloned.1.call-update) | async-done | bytes 7340048 | tf_op jit(solution)/shard_map/all_gather | solution.py:29
  100.9 3.4 broadcast_select_fusion
  104.3 0.0 copy-start.1
  104.3 0.0 copy-start.2
  104.3 0.0 all-reduce.3.cloned.1.call-update
  104.3 0.6 copy-done.1
  104.9 25.4 %all-gather = s32[16,1,128]{2,1,0:T(1,128)S(1)} all-gather(s32[1,1,128]{2,1,0:T(1,128)S(1)} %bitcast.5), channel_id=1, replica_groups=mesh['dp'=2,'ctx'=8,'feat'=16] {'dp','ctx'}, dimensions={0}, use_global_device_ids=true | all-gather | bytes 8704 | tf_op jit(solution)/shard_map/all_gather | solution.py:31
  130.3 0.0 copy-done.2
  130.3 0.1 select_reduce_fusion
  130.4 399.4 %all-reduce.3.cloned.1.call-done = (bf16[2048,1792]{1,0:T(8,128)(2,1)}, bf16[2048,512]{1,0:T(8,128)(2,1)}) async-done(((bf16[2048,1792]{1,0:T(8,128)(2,1)}, bf16[2048,512]{1,0:T(8,128)(2,1)}), (bf16[2048,1792]{1,0:T(8,128)(2,1)}, bf16[2048,512]{1,0:T(8,128)(2,1)})) %all-reduce.3.cloned.1.call-update) | async-done | bytes 9437200 | tf_op jit(solution)/shard_map/psum | solution.py:9
  529.8 0.0 copy-start
  529.8 0.0 copy-start.3
  529.8 20.7 %multiply_convert_fusion.1 = bf16[1792,1792]{1,0:T(8,128)(2,1)} fusion(bf16[2048,1792]{1,0:T(8,128)(2,1)} %get-tuple-element.2, bf16[2048,1792]{1,0:T(8,128)(2,1)} %all-gather.4.cloned.1.call-done, f32[2048]{0:T(1024)S(1)} %convert_element_type.26), kind=kOutput, calls=%fused_computation.1 | convolution fusion | flops 13170769920 | bytes 21110784 | tf_op jit(solution)/shard_map/dot_general | solution.py:20
  550.5 0.0 copy-done
  550.5 0.0 copy-done.3
  550.5 2.1 fusion.4
  (1 shorter events, 0.0 us)
Async XLA Ops:
  7.2 41.2 %all-gather.6.cloned.1.call-start = ((), (), s32[]{:S(2)}) async-start(), calls=%async_computation.1 | async-start | bytes 2228224 | tf_op jit(solution)/shard_map/all_gather | solution.py:30
  7.9 93.0 %all-gather.4.cloned.1.call-start = ((), (), s32[]{:S(2)}) async-start(), calls=%async_computation | async-start | bytes 7798784 | tf_op jit(solution)/shard_map/all_gather | solution.py:29
  8.6 521.1 %all-reduce.3.cloned.1.call-start = ((), (), s32[]{:S(2)}) async-start(), calls=%async_computation.2 | async-start | bytes 18874368 | tf_op jit(solution)/shard_map/psum | solution.py:9
  104.3 0.7 copy-start.1
  104.3 26.0 %copy-start.2 = (s32[8]{0:T(128)S(1)}, s32[8]{0:T(128)}, u32[]{:S(2)}) copy-start(s32[8]{0:T(128)} %param.7) | copy-start | bytes 100
  529.8 20.7 %copy-start = (bf16[2048,512]{1,0:T(8,128)(2,1)S(1)}, bf16[2048,512]{1,0:T(8,128)(2,1)}, u32[]{:S(2)}) copy-start(bf16[2048,512]{1,0:T(8,128)(2,1)} %all-gather.6.cloned.1.call-done) | copy-start | bytes 6291460
  529.8 20.7 %copy-start.3 = (bf16[2048,512]{1,0:T(8,128)(2,1)S(1)}, bf16[2048,512]{1,0:T(8,128)(2,1)}, u32[]{:S(2)}) copy-start(bf16[2048,512]{1,0:T(8,128)(2,1)} %get-tuple-element.3) | copy-start | bytes 6291460
Sparse Core Ops, SparseCore 0:
  9.9 38.4 all-gather.5
  50.2 50.6 all-gather.3
  104.4 425.3 all-reduce.2
where the time goes:
time: 559 us
  waiting for transfers between devices  491 us (88%)
  blocking collectives  25.4 us (5%)
  matrix products  22.9 us (4%)
  between operations  13.8 us (2%)
    psum x1, waiting for transfers between devices, from_root(): return lax.psum(block, axis)  399 us
    all_gather x1, waiting for transfers between devices, local(): lax.all_gather(out_grads, ('dp', 'ctx'), axis=0, tiled=True)  51.1 us
    all_gather x1, waiting for transfers between devices, local(): lax.all_gather(acts, ('dp', 'ctx'), axis=0, tiled=True)  39.6 us
    all_gather x1, blocking collectives, local(): lax.all_gather(domain_ids, ('dp', 'ctx'), axis=0, tiled=True)  25.4 us
    dot_general x2, matrix products, contract_tokens(): lax.dot_general(left, right, (((0,), (0,)), ((), ())), preferred_element_...  22.9 us
  transfers between devices with their start and end apart: 3, of which 3 were waited for; matrix products, arithmetic and copies ran while one was open for 0% of the time, Pallas kernels for 0%

commit v1 on v0

--- a/solution.py
+++ b/solution.py
@@ -2,6 +2,13 @@
 import jax.numpy as jnp
 from jax import lax
 from jax.sharding import PartitionSpec as P
+
+
+def swapped_in(x, axis, dim):
+    devices = lax.axis_size(axis)
+    blocks = jnp.stack([x for _ in range(devices)])
+    blocks = lax.all_to_all(blocks, axis, split_axis=0, concat_axis=0)
+    return jnp.concatenate(blocks, axis=dim)
 
 
 def from_root(block, axis, owner):
@@ -27,7 +34,7 @@
     inv_count = 1.0 / (out_grads.shape[0] * group_size)
     all_grads, all_acts, all_ids = (
         lax.all_gather(out_grads, ("dp", "ctx"), axis=0, tiled=True),
-        lax.all_gather(acts, ("dp", "ctx"), axis=0, tiled=True),
+        swapped_in(acts, ("dp", "ctx"), 0),
         lax.all_gather(domain_ids, ("dp", "ctx"), axis=0, tiled=True),
     )
     tile_ratio = lax.axis_size("feat") // group_size

time: 559 us -> 540 us (0.966)
  waiting for transfers between devices: 491 us -> 462 us
  starting transfers between devices: 0.11 us -> 6.22 us
    all_gather x1 -> x0, waiting for transfers between devices: 39.6 us -> none  [local(): lax.all_gather(acts, ('dp', 'ctx'), axis=0, tiled=True)]
    all_to_all x0 -> x1, waiting for transfers between devices: none -> 34 us  [swapped_in(): blocks = lax.all_to_all(blocks, axis, split_axis=0, concat_axis=0)]
    all_gather x1, waiting for transfers between devices: 51.1 us -> 25.8 us  [local(): lax.all_gather(out_grads, ('dp', 'ctx'), axis=0, tiled=True)]
    all_to_all x0 -> x1, starting transfers between devices: none -> 6.15 us  [swapped_in(): blocks = lax.all_to_all(blocks, axis, split_axis=0, concat_axis=0)]
  transfers between devices with their start and end apart: 3 -> 3, of which waited for: 3 -> 3; matrix products, arithmetic and copies ran while one was open for 0% -> 1% of each run, Pallas kernels for 0% -> 0%
where the time goes in v1:
time: 540 us
  waiting for transfers between devices  462 us (86%)
  blocking collectives  25.3 us (5%)
  matrix products  24.3 us (4%)
  between operations  14.1 us (3%)
  starting transfers between devices  6.22 us (1%)
    psum x1, waiting for transfers between devices, from_root(): return lax.psum(block, axis)  402 us
    all_to_all x1, waiting for transfers between devices, swapped_in(): blocks = lax.all_to_all(blocks, axis, split_axis=0, concat_axis=0)  34 us
    all_gather x1, waiting for transfers between devices, local(): lax.all_gather(out_grads, ('dp', 'ctx'), axis=0, tiled=True)  25.8 us
    all_gather x1, blocking collectives, local(): lax.all_gather(domain_ids, ('dp', 'ctx'), axis=0, tiled=True)  25.3 us
    dot_general x2, matrix products, contract_tokens(): lax.dot_general(left, right, (((0,), (0,)), ((), ())), preferred_element_...  24.3 us
  transfers between devices with their start and end apart: 3, of which 3 were waited for; matrix products, arithmetic and copies ran while one was open for 1% of the time, Pallas kernels for 0%

profile of v1, /device:TPU:41, one launch (start us, length us, event | category | flops | bytes accessed | tf_op | source)
XLA Modules:
  0.0 540.2 jit_solution(52417833540150488)
XLA Ops:
  7.2 0.0 all-gather.3.cloned.1.call-start
  7.2 0.7 all-gather.3.cloned.1.call-update
  7.9 2.4 stack.2
  10.3 6.1 %all-to-all-start = ((bf16[16,128,512]{2,1,0:T(8,128)(2,1)}), bf16[16,128,512]{2,1,0:T(8,128)(2,1)S(1)}, u32[]{:S(2)}, u32[]{:S(2)}) async-start(bf16[16,128,512]{2,1,0:T(8,128)(2,1)} %stack.2), calls=%async_computation | async-start | bytes 4194304 | tf_op jit(solution)/shard_map/all_to_all | solution.py:10
  16.5 0.0 all-reduce.3.cloned.1.call-start
  16.5 34.0 %all-to-all-done = bf16[16,128,512]{2,1,0:T(8,128)(2,1)S(1)} async-done(((bf16[16,128,512]{2,1,0:T(8,128)(2,1)}), bf16[16,128,512]{2,1,0:T(8,128)(2,1)S(1)}, u32[]{:S(2)}, u32[]{:S(2)}) %all-to-all-start) | async-done | bytes 2097184 | tf_op jit(solution)/shard_map/all_to_all | solution.py:10
  50.5 1.5 broadcast_select_fusion.1
  52.0 25.8 %all-gather.3.cloned.1.call-done = bf16[2048,1792]{1,0:T(8,128)(2,1)} async-done(((bf16[128,1792]{1,0:T(8,128)(2,1)}), bf16[2048,1792]{1,0:T(8,128)(2,1)}) %all-gather.3.cloned.1.call-update) | async-done | bytes 7340048 | tf_op jit(solution)/shard_map/all_gather | solution.py:36
  77.8 3.4 broadcast_select_fusion
  81.2 0.0 copy-start
  81.2 0.0 copy-start.1
  81.2 0.0 all-reduce.3.cloned.1.call-update
  81.3 0.6 copy-done
  81.9 25.3 %all-gather = s32[16,1,128]{2,1,0:T(1,128)S(1)} all-gather(s32[1,1,128]{2,1,0:T(1,128)S(1)} %bitcast.10), channel_id=1, replica_groups=mesh['dp'=2,'ctx'=8,'feat'=16] {'dp','ctx'}, dimensions={0}, use_global_device_ids=true | all-gather | bytes 8704 | tf_op jit(solution)/shard_map/all_gather | solution.py:38
  107.2 0.0 copy-done.1
  107.2 0.1 select_reduce_fusion
  107.3 401.7 %all-reduce.3.cloned.1.call-done = (bf16[2048,1792]{1,0:T(8,128)(2,1)}, bf16[2048,512]{1,0:T(8,128)(2,1)}) async-done(((bf16[2048,1792]{1,0:T(8,128)(2,1)}, bf16[2048,512]{1,0:T(8,128)(2,1)}), (bf16[2048,1792]{1,0:T(8,128)(2,1)}, bf16[2048,512]{1,0:T(8,128)(2,1)})) %all-reduce.3.cloned.1.call-update) | async-done | bytes 9437200 | tf_op jit(solution)/shard_map/psum | solution.py:16
  509.1 3.7 fusion.8
  512.8 20.6 %multiply_convert_fusion.1 = bf16[1792,1792]{1,0:T(8,128)(2,1)} fusion(bf16[2048,1792]{1,0:T(8,128)(2,1)} %get-tuple-element.2, bf16[2048,1792]{1,0:T(8,128)(2,1)} %all-gather.3.cloned.1.call-done, f32[2048]{0:T(1024)S(1)} %convert_element_type.29), kind=kOutput, calls=%fused_computation.1 | convolution fusion | flops 13170769920 | bytes 21110784 | tf_op jit(solution)/shard_map/dot_general | solution.py:27
  (1 shorter events, 0.0 us)
Async XLA Ops:
  7.2 70.6 %all-gather.3.cloned.1.call-start = ((), (), s32[]{:S(2)}) async-start(), calls=%async_computation.1 | async-start | bytes 7798784 | tf_op jit(solution)/shard_map/all_gather | solution.py:36
  10.3 40.2 %all-to-all-start = ((bf16[16,128,512]{2,1,0:T(8,128)(2,1)}), bf16[16,128,512]{2,1,0:T(8,128)(2,1)S(1)}, u32[]{:S(2)}, u32[]{:S(2)}) async-start(bf16[16,128,512]{2,1,0:T(8,128)(2,1)} %stack.2), calls=%async_computation | async-start | bytes 4194304 | tf_op jit(solution)/shard_map/all_to_all | solution.py:10
  16.5 492.6 %all-reduce.3.cloned.1.call-start = ((), (), s32[]{:S(2)}) async-start(), calls=%async_computation.2 | async-start | bytes 18874368 | tf_op jit(solution)/shard_map/psum | solution.py:16
  81.2 0.7 copy-start
  81.2 26.0 %copy-start.1 = (s32[8]{0:T(128)S(1)}, s32[8]{0:T(128)}, u32[]{:S(2)}) copy-start(s32[8]{0:T(128)} %param.7) | copy-start | bytes 100
Sparse Core Ops, SparseCore 0:
  9.8 67.9 all-gather.2
  81.4 427.6 all-reduce.2
